TPU v7x, 512 devices: a whole 4x8x8 slice. The times are simulated.
512 devices in a mesh: chan: 128 (over z, y, core), tm: 4 (over x).
Axes of the slice: x: 4, y: 8, z: 8, core: 2. Of those that a mesh axis runs over, the one named last changes fastest.
Arguments:
- visibilities: bfloat16 [4, 1024, 16384], P('tm', 'chan'), may hold values from -6 to 6
- flags: int32 [4, 1024, 2048], P('tm', 'chan'), may hold values 0 or 1
- taper: float32 [1024], P('chan'), may hold values from 0.3 to 1
- group_ids: int32 [2048], replicated, may hold values from 0 to 15
Outputs:
- spectrum: float32 [4, 16, 1024], P(None, None, 'chan')
Inputs may be any that keep to these rules, and one draw needn't show every extreme that they name: `group_ids`: each baseline's group number.
All inputs are finite; a program needn't handle non-finite values. No bound on the sum of `flags` on one device may be relied on, other than what follows from the above.
Results may differ from a plain program's by a relative error of at most 0.0051.
Values may be sent and summed in bfloat16 or wider, within the bound.
No kernel may reach another device: no remote copies, remote signals or barrier semaphores. Data moves between devices by JAX's collectives and lax.ppermute only.
A program may use at most 64 MiB of HBM per device.

v0:
```python
import math
import jax
import jax.numpy as jnp
from jax import lax
from jax.sharding import PartitionSpec as P

G = 16


def tables(length):
    positions = jnp.arange(length, dtype=jnp.int32)
    product = positions[:, None] * positions[None, :] % length
    phases = product.astype(jnp.float32) * (2.0 * math.pi / length)
    normalizing_scale = 1.0 / math.sqrt(length)
    return (
        (jnp.cos(phases) * normalizing_scale).astype(jnp.bfloat16),
        (jnp.sin(phases) * normalizing_scale).astype(jnp.bfloat16),
    )


def body(visibilities, flags, taper, group_ids):
    local_times, local_chans, column_entries = visibilities.shape
    baseline_pairs = column_entries // 8
    channels = local_chans * lax.axis_size("chan")
    shard_count = baseline_pairs // lax.axis_size("chan")
    times_all = local_times * lax.axis_size("tm")
    cos_tab, sin_tab = tables(channels)
    group_range = jnp.arange(G, dtype=jnp.int32)
    shard_group_index = lax.dynamic_slice_in_dim(
        group_ids, lax.axis_index("chan") * shard_count, shard_count
    )
    group_member = (shard_group_index[None, :] == group_range[:, None]).astype(jnp.float32)
    turned = lax.all_to_all(visibilities, "chan", split_axis=2, concat_axis=1, tiled=True)
    turned_flags = lax.all_to_all(flags, "chan", split_axis=2, concat_axis=1, tiled=True)
    full_taper = lax.all_gather(taper, "chan", axis=0, tiled=True)
    weight = (1 - turned_flags).astype(jnp.float32) * full_taper[None, :, None]
    shaped = turned.reshape(local_times, channels, shard_count, 8).astype(jnp.float32)
    tapered = (
        (shaped * weight[..., None])
        .astype(jnp.bfloat16)
        .reshape(local_times, channels, shard_count * 8)
    )
    items = tapered.shape[0]
    cosine_part = jnp.einsum(
        "dc,tcn->tdn", cos_tab, tapered, preferred_element_type=jnp.float32
    ).reshape(items, channels, shard_count, 4, 2)
    sine_part = jnp.einsum(
        "dc,tcn->tdn", sin_tab, tapered, preferred_element_type=jnp.float32
    ).reshape(items, channels, shard_count, 4, 2)
    real_part = cosine_part[..., 0] + sine_part[..., 1]
    imag_part = cosine_part[..., 1] - sine_part[..., 0]
    group_real = jnp.einsum(
        "tdbs,gb->tsgd", real_part, group_member, precision=lax.Precision.HIGHEST
    )
    group_imag = jnp.einsum(
        "tdbs,gb->tsgd", imag_part, group_member, precision=lax.Precision.HIGHEST
    )
    autocorrelation_terms = jnp.einsum(
        "tdbs,gb->tsgd",
        real_part * real_part + imag_part * imag_part,
        group_member,
        precision=lax.Precision.HIGHEST,
    )
    group_terms = jnp.stack([group_real, group_imag, autocorrelation_terms], axis=1)
    owned = lax.psum_scatter(group_terms, "chan", scatter_dimension=4, tiled=True)
    spectrum = jnp.sum(owned[:, 0] * owned[:, 0] + owned[:, 1] * owned[:, 1] - owned[:, 2], axis=0)
    spectrum = lax.psum(spectrum, "tm")
    member_all = (group_ids[None, :] == group_range[:, None]).astype(jnp.float32)
    counts = jnp.sum(member_all, axis=1)
    pair_count = jnp.maximum(counts * (counts - 1.0), 1.0)
    return spectrum / jnp.sqrt(pair_count * times_all)[None, :, None]


def solution(mesh):
    return jax.shard_map(
        body,
        mesh=mesh,
        in_specs=(P("tm", "chan", None), P("tm", "chan", None), P("chan"), P()),
        out_specs=P(None, None, "chan"),
        check_vma=False,
    )
```

profile of v0, /device:TPU:24, one launch (start us, length us, event | category | flops | bytes accessed | tf_op | source)
XLA Modules:
  0.0 725.1 jit_solution(13528118081946566250)
XLA Ops:
  6.5 1.9 copy.69
  8.9 9.3 %reduce = s32[2048,8]{1,0:T(8,128)S(1)} reduce(s32[2048,1,8]{2,1,0:T(1,128)S(1)} %bitcast.79, s32[]{:T(128)} %broadcast.92), dimensions={1}, to_apply=%bitcast.69.reduce_sub_computation | reduce | bytes 131076
  18.3 1.1 reshape.135
  19.4 17.1 %all-to-all-start.1 = ((s32[128,1,128]{2,1,0:T(1,128)}), s32[128,1,128]{2,1,0:T(1,128)S(1)}, u32[]{:S(2)}, u32[]{:S(2)}) async-start(s32[128,1,128]{2,1,0:T(1,128)} %reshape.135), calls=%async_computation.1 | async-start | bytes 131072 | tf_op jit(solution)/shard_map/all_to_all | solution.py:34
  36.6 12.7 %copy.66 = bf16[1,8,16384]{1,0,2:T(2,128)(2,1)} copy(bf16[1,8,16384]{2,1,0:T(8,128)(2,1)S(1)} %copy-done) | data formatting | bytes 524288 | tf_op args[0]
  49.8 90.8 %reduce.2 = bf16[16384,8]{1,0:T(8,128)(2,1)} reduce(bf16[16384,1,8]{2,1,0:T(2,128)(2,1)} %bitcast.77, bf16[]{:T(256)} %broadcast.94), dimensions={1}, to_apply=%bitcast.71.reduce_sub_computation | reduce | bytes 524290
  140.6 6.9 reshape.137
  147.5 0.6 fusion.48
  149.1 237.0 %all-reduce = f32[1024]{0:T(1024)S(1)} all-reduce(f32[1024]{0:T(1024)S(1)} %dynamic-update-slice), channel_id=1, replica_groups=mesh['chan'=128,'tm'=4] {'chan'}, use_global_device_ids=true, to_apply=%add | all-reduce | flops 1024 | bytes 8192
  386.1 21.1 %all-to-all-start = ((bf16[128,2,512]{2,1,0:T(2,128)(2,1)}), bf16[128,2,512]{2,1,0:T(2,128)(2,1)S(1)}, u32[]{:S(2)}, u32[]{:S(2)}) async-start(bf16[128,2,512]{2,1,0:T(2,128)(2,1)} %reshape.137), calls=%async_computation | async-start | bytes 524288 | tf_op jit(solution)/shard_map/all_to_all | solution.py:33
  407.4 0.8 reduce.1
  408.2 1.6 reshape.136
  411.3 8.6 %all-to-all-done = bf16[128,2,512]{2,1,0:T(2,128)(2,1)S(1)} async-done(((bf16[128,2,512]{2,1,0:T(2,128)(2,1)}), bf16[128,2,512]{2,1,0:T(2,128)(2,1)S(1)}, u32[]{:S(2)}, u32[]{:S(2)}) %all-to-all-start) | async-done | bytes 262176 | tf_op jit(solution)/shard_map/all_to_all | solution.py:33
  420.0 17.1 %reshape.138 = bf16[16384,1,8]{2,1,0:T(2,128)(2,1)} reshape(bf16[128,2,512]{2,1,0:T(2,128)(2,1)S(1)} %all-to-all-done) | data formatting | bytes 524288
  437.1 14.8 %copy.67 = bf16[1,8,16384]{2,1,0:T(8,128)(2,1)S(1)} copy(bf16[1,8,16384]{1,0,2:T(2,128)(2,1)} %bitcast.78) | data formatting | bytes 524288 | tf_op jit(solution)/shard_map/all_to_all | solution.py:33
  452.3 16.1 %fusion.13 = f32[1,1024,128]{1,2,0:T(8,128)S(1)} fusion(bf16[1024,128]{1,0:T(8,128)(2,1)S(1)} %fusion.14), kind=kOutput, calls=%fused_computation.16 | convolution fusion | flops 285212672 | bytes 786432 | tf_op jit(solution)/shard_map/dc,tcn->tdn/dot_general | solution.py:44
  468.4 16.5 %fusion.12 = f32[1,1024,128]{1,2,0:T(8,128)S(1)} fusion(bf16[1024,128]{1,0:T(8,128)(2,1)S(1)} %fusion.14), kind=kOutput, calls=%fused_computation.15 | convolution fusion | flops 285212672 | bytes 786432 | tf_op jit(solution)/shard_map/dc,tcn->tdn/dot_general | solution.py:47
  485.5 1.2 fusion.46
  487.3 1.1 convolution_bitcast_fusion
  489.0 4.6 copy.78
  494.4 205.7 %all-reduce.4.cloned.1.call-done = f32[1,3,4,16,1024]{3,2,1,0,4:T(4,128)} async-done(((f32[1,3,4,16,1024]{3,2,1,0,4:T(4,128)}), f32[1,3,4,16,1024]{3,2,1,0,4:T(4,128)}) %all-reduce.4.cloned.1.call-update) | async-done | bytes 786448
  700.1 0.8 constant_dynamic-slice_fusion.1
  700.9 16.8 %psum.7 = f32[4,16,8]{1,2,0:T(8,128)S(1)} all-reduce(f32[4,16,8]{1,2,0:T(8,128)S(1)} %fusion.24), channel_id=1, replica_groups=mesh['chan'=128,'tm'=4] {'tm'}, use_global_device_ids=true, to_apply=%region_1.2 | all-reduce | flops 512 | bytes 4096 | tf_op jit(solution)/shard_map/psum | solution.py:67
  717.7 0.6 broadcast_divide_fusion
  (34 shorter events, 5.6 us)
Async XLA Ops:
  6.5 30.1 %copy-start = (bf16[1,8,16384]{2,1,0:T(8,128)(2,1)S(1)}, bf16[1,8,16384]{2,1,0:T(8,128)(2,1)}, u32[]{:S(2)}) copy-start(bf16[1,8,16384]{2,1,0:T(8,128)(2,1)} %param.4) | copy-start | bytes 786436
  19.4 366.6 %all-to-all-start.1 = ((s32[128,1,128]{2,1,0:T(1,128)}), s32[128,1,128]{2,1,0:T(1,128)S(1)}, u32[]{:S(2)}, u32[]{:S(2)}) async-start(s32[128,1,128]{2,1,0:T(1,128)} %reshape.135), calls=%async_computation.1 | async-start | bytes 131072 | tf_op jit(solution)/shard_map/all_to_all | solution.py:34
  140.6 6.9 copy-start.2
  140.6 8.2 %copy-start.1 = (s32[2048]{0:T(1024)S(1)}, s32[2048]{0:T(1024)}, u32[]{:S(2)}) copy-start(s32[2048]{0:T(1024)} %param.7) | copy-start | bytes 24580
  140.6 8.3 %copy-start.3 = (f32[8]{0:T(128)S(1)}, f32[8]{0:T(128)}, u32[]{:S(2)}) copy-start(f32[8]{0:T(128)} %param.6) | copy-start | bytes 100
  386.1 33.9 %all-to-all-start = ((bf16[128,2,512]{2,1,0:T(2,128)(2,1)}), bf16[128,2,512]{2,1,0:T(2,128)(2,1)S(1)}, u32[]{:S(2)}, u32[]{:S(2)}) async-start(bf16[128,2,512]{2,1,0:T(2,128)(2,1)} %reshape.137), calls=%async_computation | async-start | bytes 524288 | tf_op jit(solution)/shard_map/all_to_all | solution.py:33
  407.1 292.9 %all-reduce.4.cloned.1.call-start = ((), (), s32[]{:S(2)}) async-start(), calls=%async_computation.2 | async-start | bytes 12582912
Sparse Core Ops, SparseCore 0:
  493.8 206.2 all-reduce.3
where the time goes:
time: 726 us; the launch traced here: 725 us
  blocking collectives  254 us (35%)
  waiting for transfers between devices  214 us (29%)
  other arithmetic  102 us (14%)
  local copies, waits for them, and re-layouts  66.5 us (9%)
  starting transfers between devices  38.5 us (5%)
  matrix products  34.8 us (5%)
  between operations  14.9 us (2%)
    unnamed x1, blocking collectives  237 us
    unnamed x2, waiting for transfers between devices  206 us
    unnamed x3, other arithmetic  100 us
    unnamed x20, local copies, waits for them, and re-layouts  43.4 us
    all_to_all x1, starting transfers between devices, body(): lax.all_to_all(visibilities, 'chan', split_axis=2, concat_axis=1, tiled=T...  21.1 us
    all_to_all x1, starting transfers between devices, body(): lax.all_to_all(flags, 'chan', split_axis=2, concat_axis=1, tiled=True)  17.1 us
    psum x1, blocking collectives, body(): spectrum = lax.psum(spectrum, 'tm')  16.8 us
    dot_general x1, matrix products, body(): jnp.einsum('dc,tcn->tdn', sin_tab, tapered, preferred_element_type=jnp.fl...  16.5 us
  transfers between devices with their start and end apart: 3, of which 2 were waited for; matrix products, arithmetic and copies ran while one was open for 16% of the time, Pallas kernels for 0%

commit v1 on v0

--- a/solution.py
+++ b/solution.py
@@ -3,8 +3,18 @@
 import jax.numpy as jnp
 from jax import lax
 from jax.sharding import PartitionSpec as P
+from jax.lax import all_to_all, axis_size
 
 G = 16
+press_values = lambda in_array, d0, ndim_at: jnp.concatenate(
+    all_to_all(
+        jnp.stack(jnp.split(in_array, axis_size("chan"), axis=ndim_at), axis=0),
+        axis_name="chan",
+        split_axis=0,
+        concat_axis=0,
+    ),
+    axis=d0,
+)
 
 
 def tables(length):
@@ -30,7 +40,7 @@
         group_ids, lax.axis_index("chan") * shard_count, shard_count
     )
     group_member = (shard_group_index[None, :] == group_range[:, None]).astype(jnp.float32)
-    turned = lax.all_to_all(visibilities, "chan", split_axis=2, concat_axis=1, tiled=True)
+    turned = press_values(visibilities, 1, 2)
     turned_flags = lax.all_to_all(flags, "chan", split_axis=2, concat_axis=1, tiled=True)
     full_taper = lax.all_gather(taper, "chan", axis=0, tiled=True)
     weight = (1 - turned_flags).astype(jnp.float32) * full_taper[None, :, None]

time: 726 us -> 665 us (0.916); the launches traced: 725 us -> 656 us
  other arithmetic: 102 us -> 11.3 us
  local copies, waits for them, and re-layouts: 66.5 us -> 89.1 us
    unnamed x3 -> x1, other arithmetic: 100 us -> 9.34 us
    unnamed x20 -> x142, local copies, waits for them, and re-layouts: 43.4 us -> 80 us
    all_to_all x1 -> x0, local copies, waits for them, and re-layouts: 14.8 us -> none  [body(): lax.all_to_all(visibilities, 'chan', split_axis=2, concat_axis=1, tiled=T...]
  transfers between devices with their start and end apart: 3 -> 3, of which waited for: 2 -> 2; matrix products, arithmetic and copies ran while one was open for 16% -> 12% of each run, Pallas kernels for 0% -> 0%
where the time goes in v1:
time: 665 us; the launch traced here: 656 us
  blocking collectives  254 us (38%)
  waiting for transfers between devices  214 us (32%)
  local copies, waits for them, and re-layouts  89.1 us (13%)
  starting transfers between devices  38.2 us (6%)
  matrix products  34.3 us (5%)
  between operations  15.2 us (2%)
  other arithmetic  11.3 us (2%)
    unnamed x1, blocking collectives  237 us
    unnamed x2, waiting for transfers between devices  206 us
    unnamed x142, local copies, waits for them, and re-layouts  80 us
    all_to_all x1, starting transfers between devices, all_to_all(jnp.stack(jnp.split(in_array, axis_size('chan'), axis=ndim_at)...  21.1 us
    all_to_all x1, starting transfers between devices, body(): lax.all_to_all(flags, 'chan', split_axis=2, concat_axis=1, tiled=True)  17.1 us
    psum x1, blocking collectives, body(): spectrum = lax.psum(spectrum, 'tm')  16.8 us
    dot_general x1, matrix products, body(): jnp.einsum('dc,tcn->tdn', cos_tab, tapered, preferred_element_type=jnp.fl...  16.1 us
    dot_general x1, matrix products, body(): jnp.einsum('dc,tcn->tdn', sin_tab, tapered, preferred_element_type=jnp.fl...  16 us
  transfers between devices with their start and end apart: 3, of which 2 were waited for; matrix products, arithmetic and copies ran while one was open for 12% of the time, Pallas kernels for 0%

profile of v1, /device:TPU:24, one launch (start us, length us, event | category | flops | bytes accessed | tf_op | source)
XLA Modules:
  0.0 656.3 jit_solution(16165732554115645789)
XLA Ops:
  6.5 1.9 copy.51
  9.0 9.3 %reduce = s32[2048,8]{1,0:T(8,128)S(1)} reduce(s32[2048,1,8]{2,1,0:T(1,128)S(1)} %bitcast.321, s32[]{:T(128)} %broadcast.92), dimensions={1}, to_apply=%bitcast.319.reduce_sub_computation | reduce | bytes 131076
  18.3 1.1 reshape.130
  19.4 17.1 %all-to-all-start.1 = ((s32[128,1,128]{2,1,0:T(1,128)}), s32[128,1,128]{2,1,0:T(1,128)S(1)}, u32[]{:S(2)}, u32[]{:S(2)}) async-start(s32[128,1,128]{2,1,0:T(1,128)} %reshape.130), calls=%async_computation.1 | async-start | bytes 131072 | tf_op jit(solution)/shard_map/all_to_all | solution.py:44
  36.6 0.7 fusion.50
  38.2 237.0 %all-reduce = f32[1024]{0:T(1024)S(1)} all-reduce(f32[1024]{0:T(1024)S(1)} %dynamic-update-slice), channel_id=1, replica_groups=mesh['chan'=128,'tm'=4] {'chan'}, use_global_device_ids=true, to_apply=%add | all-reduce | flops 1024 | bytes 8192
  282.8 0.6 constant_dynamic-update-slice_fusion.114
  286.9 0.6 constant_dynamic-update-slice_fusion.107
  300.3 0.6 constant_dynamic-update-slice_fusion.84
  317.2 0.6 constant_dynamic-update-slice_fusion.55
  349.9 21.1 %all-to-all-start = ((bf16[128,1,8,128]{3,2,1,0:T(8,128)(2,1)}), bf16[128,1,8,128]{3,2,1,0:T(8,128)(2,1)S(1)}, u32[]{:S(2)}, u32[]{:S(2)}) async-start(bf16[128,1,8,128]{3,2,1,0:T(8,128)(2,1)} %constant_dynamic-update-slice_fusion), calls=%async_computation | async-start | bytes 524288 | tf_op jit(solution)/shard_map/all_to_all | solution.py:10
  371.0 0.8 reduce.1
  371.8 1.6 reshape.131
  373.4 0.7 copy.52
  375.1 8.7 %all-to-all-done = bf16[128,1,8,128]{3,2,1,0:T(8,128)(2,1)S(1)} async-done(((bf16[128,1,8,128]{3,2,1,0:T(8,128)(2,1)}), bf16[128,1,8,128]{3,2,1,0:T(8,128)(2,1)S(1)}, u32[]{:S(2)}, u32[]{:S(2)}) %all-to-all-start) | async-done | bytes 262176 | tf_op jit(solution)/shard_map/all_to_all | solution.py:10
  383.8 16.1 %fusion.13 = f32[1,1024,128]{1,2,0:T(8,128)S(1)} fusion(f32[1024,128]{1,0:T(8,128)S(1)} %copy.55, bf16[128,1,8,128]{3,2,1,0:T(8,128)(2,1)S(1)} %all-to-all-done), kind=kOutput, calls=%fused_computation.16 | convolution fusion | flops 285605888 | bytes 1310720 | tf_op jit(solution)/shard_map/dc,tcn->tdn/dot_general | solution.py:54
  400.2 16.0 %fusion.12 = f32[1,1024,128]{1,2,0:T(8,128)S(1)} fusion(f32[1024,128]{1,0:T(8,128)S(1)} %copy.55, bf16[128,1,8,128]{3,2,1,0:T(8,128)(2,1)S(1)} %all-to-all-done), kind=kOutput, calls=%fused_computation.15 | convolution fusion | flops 285605888 | bytes 1310720 | tf_op jit(solution)/shard_map/dc,tcn->tdn/dot_general | solution.py:57
  416.5 1.2 fusion.48
  418.2 1.1 convolution_bitcast_fusion
  420.0 4.6 copy.60
  425.4 205.7 %all-reduce.4.cloned.1.call-done = f32[1,3,4,16,1024]{3,2,1,0,4:T(4,128)} async-done(((f32[1,3,4,16,1024]{3,2,1,0,4:T(4,128)}), f32[1,3,4,16,1024]{3,2,1,0,4:T(4,128)}) %all-reduce.4.cloned.1.call-update) | async-done | bytes 786448
  631.0 0.8 constant_dynamic-slice_fusion.1
  631.8 16.8 %psum.7 = f32[4,16,8]{1,2,0:T(8,128)S(1)} all-reduce(f32[4,16,8]{1,2,0:T(8,128)S(1)} %fusion.24), channel_id=1, replica_groups=mesh['chan'=128,'tm'=4] {'tm'}, use_global_device_ids=true, to_apply=%region_1.2 | all-reduce | flops 512 | bytes 4096 | tf_op jit(solution)/shard_map/psum | solution.py:77
  648.6 0.6 broadcast_divide_fusion
  (153 shorter events, 76.0 us)
Async XLA Ops:
  6.5 30.1 %copy-start.2 = (u32[512]{0:T(512)S(1)}, u32[512]{0:T(512)}, u32[]{:S(2)}) copy-start(u32[512]{0:T(512)} %constant.45) | copy-start | bytes 6148
  6.5 31.5 %copy-start.3 = (f32[8]{0:T(128)S(1)}, f32[8]{0:T(128)}, u32[]{:S(2)}) copy-start(f32[8]{0:T(128)} %param.6) | copy-start | bytes 100
  6.5 268.7 %copy-start = (bf16[1,8,16384]{2,1,0:T(8,128)(2,1)S(1)}, bf16[1,8,16384]{2,1,0:T(8,128)(2,1)}, u32[]{:S(2)}) copy-start(bf16[1,8,16384]{2,1,0:T(8,128)(2,1)} %param.4) | copy-start | bytes 786436
  6.5 342.7 %copy-start.1 = (s32[2048]{0:T(1024)S(1)}, s32[2048]{0:T(1024)}, u32[]{:S(2)}) copy-start(s32[2048]{0:T(1024)} %param.7) | copy-start | bytes 24580
  19.4 330.4 %all-to-all-start.1 = ((s32[128,1,128]{2,1,0:T(1,128)}), s32[128,1,128]{2,1,0:T(1,128)S(1)}, u32[]{:S(2)}, u32[]{:S(2)}) async-start(s32[128,1,128]{2,1,0:T(1,128)} %reshape.130), calls=%async_computation.1 | async-start | bytes 131072 | tf_op jit(solution)/shard_map/all_to_all | solution.py:44
  349.9 33.9 %all-to-all-start = ((bf16[128,1,8,128]{3,2,1,0:T(8,128)(2,1)}), bf16[128,1,8,128]{3,2,1,0:T(8,128)(2,1)S(1)}, u32[]{:S(2)}, u32[]{:S(2)}) async-start(bf16[128,1,8,128]{3,2,1,0:T(8,128)(2,1)} %constant_dynamic-update-slice_fusion), calls=%async_computation | async-start | bytes 524288 | tf_op jit(solution)/shard_map/all_to_all | solution.py:10
  370.9 260.1 %all-reduce.4.cloned.1.call-start = ((), (), s32[]{:S(2)}) async-start(), calls=%async_computation.2 | async-start | bytes 12582912
Sparse Core Ops, SparseCore 0:
  424.7 206.2 all-reduce.3
